TPU v7x, 32 devices: a whole 2x2x4 slice. The times are simulated.
32 devices in a mesh: grp: 2 (over y), seq: 4 (over z), head: 4 (over x, core).
Axes of the slice: x: 2, y: 2, z: 4, core: 2. Of those that a mesh axis runs over, the one named last changes fastest.
Arguments:
- lin_query: bfloat16 [2560, 8192], P(('grp', 'seq'), 'head'), parts along dimension 0, may hold values from -6 to 6
- lin_key: bfloat16 [2560, 8192], P(('grp', 'seq'), 'head'), parts along dimension 0, may hold values from -6 to 6
- lin_value: bfloat16 [2560, 8192], P(('grp', 'seq'), 'head'), parts along dimension 0, may hold values from -6 to 6
- norm_gain: bfloat16 [8192], P('head'), may hold values from 0.25 to 1.75
- out_gate: bfloat16 [2560, 8192], P(('grp', 'seq'), 'head'), parts along dimension 0, may hold values from -6 to 6
- soft_query: bfloat16 [2560, 8192], P(('grp', 'seq'), 'head'), parts along dimension 0, may hold values from -24 to 24
- soft_key: bfloat16 [2560, 8192], P(('grp', 'seq'), 'head'), parts along dimension 0, may hold values from -24 to 24
- doc_id: int32 [2560], P(('grp', 'seq')), parts along dimension 0, may hold values from 0 to 7, never falling along the last dimension, each value on 1 to 640 neighbouring positions
Outputs:
- lin_out: bfloat16 [2560, 8192], P(('grp', 'seq'), 'head'), parts along dimension 0
- soft_out: bfloat16 [2560, 8192], P(('grp', 'seq'), 'head'), parts along dimension 0
There are 2 independent parts, one for each index of `grp`. A program takes and returns all parts, laid end to end along the dimension named above; an argument that names none is the same for every part. Nothing has to cross between parts.
Inputs may be any that keep to these rules, and one draw needn't show every extreme that they name: `doc_id`: never falls along the sequence; every document holds 1 to half of 1280 tokens, and one holds exactly half of 1280.
All inputs are finite; a program needn't handle non-finite values.
Results may differ from a plain program's by a relative error of at most 0.0095.
Values may be sent and summed in bfloat16 or wider, within the bound.
No kernel may reach another device: no remote copies, remote signals or barrier semaphores. Data moves between devices by JAX's collectives and lax.ppermute only.
A program may use at most 192 MiB of HBM per device.

v0:
```python
import math
import jax
import jax.numpy as jnp
from jax import lax
from jax.sharding import PartitionSpec as P

HD = 128
norm_eps = 1e-06


def per_device(lin_query, lin_key, lin_value, norm_gain, out_gate, soft_query, soft_key, doc_id):
    row_count = lin_query.shape[0]
    head_count = lin_query.shape[1] // HD
    my_index = lax.axis_index("seq")
    queries = lin_query.reshape(row_count, head_count, HD)
    key_rows = lin_key.reshape(row_count, head_count, HD)
    value_rows = lin_value.reshape(row_count, head_count, HD)
    first_doc = doc_id[0]
    last_doc = doc_id[-1]
    tail_keys = jnp.where((doc_id == last_doc)[:, None, None], key_rows, jnp.zeros_like(key_rows))
    local_state = jnp.einsum(
        "thd,the->hde", tail_keys, value_rows, preferred_element_type=jnp.float32
    )
    empty_state = jnp.zeros_like(local_state)
    states = lax.all_gather(
        local_state[None].astype(jnp.bfloat16), "seq", axis=0, tiled=True
    ).astype(jnp.float32)
    tags = lax.all_gather(last_doc[None], "seq", axis=0, tiled=True)
    sources = jnp.arange(tags.shape[0], dtype=jnp.int32)
    wanted = (tags == first_doc) & (sources < my_index)
    carried = empty_state + jnp.sum(
        jnp.where(wanted[:, None, None, None], states, jnp.zeros_like(states)), axis=0
    )
    positions = jnp.arange(row_count, dtype=jnp.int32)
    causal = positions[:, None] >= positions[None, :]
    keep_local = causal & (doc_id[:, None] == doc_id[None, :])
    scores = jnp.einsum("qhd,khd->hqk", queries, key_rows, preferred_element_type=jnp.float32)
    rounded = jnp.where(keep_local[None], scores, jnp.zeros_like(scores)).astype(jnp.bfloat16)
    block_term = jnp.einsum("hqk,khd->qhd", rounded, value_rows, preferred_element_type=jnp.float32)
    carried_term = jnp.einsum(
        "qhd,hde->qhe", queries.astype(jnp.float32), carried, precision=lax.Precision.HIGHEST
    )
    carried_term = jnp.where(
        (doc_id == first_doc)[:, None, None], carried_term, jnp.zeros_like(carried_term)
    )
    lin_raw = block_term + carried_term
    mean_square = jnp.mean(lin_raw * lin_raw, axis=-1, keepdims=True)
    gain_rows = norm_gain.astype(jnp.float32).reshape(head_count, HD)
    gate_rows = jax.nn.sigmoid(out_gate.astype(jnp.float32).reshape(row_count, head_count, HD))
    normed = lin_raw * lax.rsqrt(mean_square + norm_eps) * gain_rows * gate_rows
    lin_out = normed.astype(jnp.bfloat16).reshape(row_count, head_count * HD)
    query_soft = soft_query.reshape(row_count, head_count, HD)
    query_pos = my_index * row_count + positions
    score_scale = 1.0 / math.sqrt(HD)
    key_flat = lax.all_gather(soft_key, "seq", axis=0, tiled=True)
    row_max = jnp.full((head_count, row_count), -1e30, jnp.float32)
    piece_rows = key_flat.shape[0]
    key_part = key_flat.reshape(piece_rows, head_count, HD)
    value_part = lax.all_gather(lin_out, "seq", axis=0, tiled=True).reshape(
        piece_rows, head_count, HD
    )
    key_pos = jnp.arange(piece_rows, dtype=jnp.int32)
    logits = (
        jnp.einsum("qhd,khd->hqk", query_soft, key_part, preferred_element_type=jnp.float32)
        * score_scale
    )
    keep_mask = (
        (query_pos[:, None] >= key_pos[None, :])
        & (doc_id[:, None] == lax.all_gather(doc_id, "seq", axis=0, tiled=True)[None, :])
        & True
    )
    logits = jnp.where(keep_mask[None], logits, -1e30)
    new_max = jnp.maximum(row_max, jnp.max(logits, axis=-1))
    probs = jnp.where(keep_mask[None], jnp.exp(logits - new_max[..., None]), 0.0)
    denom_sum = jnp.sum(probs, axis=-1)
    update = jnp.einsum(
        "hqk,khd->qhd", probs.astype(jnp.bfloat16), value_part, preferred_element_type=jnp.float32
    )
    soft_out = update / jnp.transpose(denom_sum)[:, :, None]
    return (lin_out, soft_out.astype(jnp.bfloat16).reshape(row_count, head_count * HD))


def solution(mesh):
    return jax.shard_map(
        per_device,
        mesh=mesh,
        in_specs=(
            P(("grp", "seq"), "head"),
            P(("grp", "seq"), "head"),
            P(("grp", "seq"), "head"),
            P("head"),
            P(("grp", "seq"), "head"),
            P(("grp", "seq"), "head"),
            P(("grp", "seq"), "head"),
            P(("grp", "seq")),
        ),
        out_specs=(P(("grp", "seq"), "head"), P(("grp", "seq"), "head")),
        check_vma=False,
    )
```

profile of v0, /device:TPU:0, one launch (start us, length us, event | category | flops | bytes accessed | tf_op | source)
XLA Modules:
  0.0 291.2 jit_solution(3869232572104715279)
XLA Ops:
  7.2 0.0 copy-start
  7.2 0.0 all-gather.9.cloned.1.call-start
  7.2 1.3 dynamic-slice
  8.6 2.0 fusion.52
  10.6 2.0 broadcast_compare_fusion.1
  12.5 0.0 copy-start.4
  12.5 0.0 copy-start.5
  12.5 3.4 %fusion.34 = bf16[16,128,128]{2,1,0:T(8,128)(2,1)} fusion(pred[320]{0:T(512)(128)(4,1)S(1)} %get-tuple-element.5, bf16[320,2048]{1,0:T(8,128)(2,1)} %param.10, bf16[320,2048]{1,0:T(8,128)(2,1)} %param.9), kind=kOutput, calls=%fused_computation.39 | convolution fusion | flops 168689664 | bytes 3146048 | tf_op jit(solution)/shard_map/thd,the->hde/dot_general | solution.py:21
  15.9 0.0 copy-start.3
  15.9 0.0 all-gather.9.cloned.1.call-update
  16.0 0.0 all-gather.7.cloned.1.call-start
  16.0 0.7 all-gather.7.cloned.1.call-update
  16.7 0.0 all-gather.5.cloned.1.call-start
  17.4 0.0 copy-done.4
  17.4 0.3 dynamic-update-slice.1
  17.7 10.1 %all-reduce.2 = (s32[4]{0:T(128)S(1)}, s32[1280]{0:T(1024)S(1)}) all-reduce(s32[4]{0:T(128)S(1)} %get-tuple-element.7, s32[1280]{0:T(1024)S(1)} %dynamic-update-slice.1), channel_id=1, replica_groups=mesh['grp'=2,'seq'=4,'head'=4] {'seq'}, use_global_device_ids=true, to_apply=%add | all-reduce | flops 1284 | bytes 10272
  27.8 0.6 compare_and_fusion
  28.5 0.0 copy-done.5
  28.5 0.1 fusion.46
  28.6 36.1 %all-gather.9.cloned.1.call-done = bf16[64,128,128]{2,1,0:T(8,128)(2,1)} async-done(((bf16[16,128,128]{2,1,0:T(8,128)(2,1)}), bf16[64,128,128]{2,1,0:T(8,128)(2,1)}) %all-gather.9.cloned.1.call-update) | async-done | bytes 2097168 | tf_op jit(solution)/shard_map/all_gather | solution.py:25
  64.8 2.2 fusion.6
  67.0 0.0 copy-done.3
  67.0 2.7 fusion.29
  69.7 0.0 copy-start.2
  69.7 7.2 %multiply_reduce_fusion = (f32[320,16]{0,1:T(8,128)S(1)}, f32[320,16,128]{2,0,1:T(8,128)}) fusion(f32[16,128,320]{1,2,0:T(8,128)} %fusion.29, pred[320]{0:T(512)(128)(4,1)S(1)} %get-tuple-element.4, pred[320,320]{1,0:T(8,128)(4,1)S(1)} %fusion.46, bf16[320,2048]{1,0:T(8,128)(2,1)} %param.10, bf16[320,2048]{1,0:T(8,128)(2,1)} %param.9, ...), kind=kOutput, calls=%fused_computation.20 | convolution fusion | flops 844753920 | bytes 9298240 | tf_op jit(solution)/shard_map/hqk,khd->qhd/dot_general | solution.py:39
  76.9 0.0 copy-done.2
  76.9 3.2 %copy_bitcast_fusion.1 = bf16[320,2048]{1,0:T(8,128)(2,1)} fusion(f32[320,16,128]{2,0,1:T(8,128)} %get-tuple-element.10, f32[16,128]{1,0:T(8,128)S(1)} %bitcast_convert_fusion, f32[320,16]{0,1:T(8,128)S(1)} %add_rsqrt_fusion, bf16[320,2048]{1,0:T(8,128)(2,1)S(1)} %copy-done.2), kind=kLoop, calls=%fused_computation.26 | loop fusion | flops 5242880 | bytes 5271552 | tf_op jit(solution)/shard_map/reshape | solution.py:51
  80.1 0.0 all-gather.5.cloned.1.call-update
  80.2 0.4 fusion.16
  80.6 82.6 %all-gather.7.cloned.1.call-done = bf16[1280,2048]{1,0:T(8,128)(2,1)} async-done(((bf16[320,2048]{1,0:T(8,128)(2,1)}), bf16[1280,2048]{1,0:T(8,128)(2,1)}) %all-gather.7.cloned.1.call-update) | async-done | bytes 5242896 | tf_op jit(solution)/shard_map/all_gather | solution.py:55
  163.1 7.9 %copy.36 = bf16[1280,2048]{0,1:T(8,128)(2,1)} copy(bf16[1280,2048]{1,0:T(8,128)(2,1)} %all-gather.7.cloned.1.call-done) | data formatting | bytes 10485760 | tf_op jit(solution)/shard_map/all_gather | solution.py:55
  171.1 0.0 copy-done
  171.1 13.3 %fusion = (f32[16,320]{1,0:T(8,128)S(1)}, f32[16,320,1280]{2,1,0:T(8,128)}) fusion(pred[320,1280]{1,0:T(8,128)(4,1)S(1)} %fusion.16, bf16[1280,16,128]{0,2,1:T(8,128)(2,1)} %bitcast.105, bf16[320,2048]{1,0:T(8,128)(2,1)S(1)} %copy-done), kind=kOutput, calls=%fused_computation.2 | convolution fusion | flops 1697377280 | bytes 33198080 | tf_op jit(solution)/shard_map/qhd,khd->hqk/dot_general | solution.py:64
  184.4 13.9 %fusion.1 = f32[16,320]{1,0:T(8,128)S(1)} fusion(f32[16,320,1280]{2,1,0:T(8,128)} %get-tuple-element.12, f32[16,320]{1,0:T(8,128)S(1)} %broadcast_maximum_fusion, pred[320,1280]{1,0:T(8,128)(4,1)S(1)} %fusion.16), kind=kLoop, calls=%fused_computation.3 | loop fusion | flops 32762880 | bytes 26664960 | tf_op jit(solution)/shard_map/reduce_sum | solution.py:75
  198.3 63.4 %all-gather.5.cloned.1.call-done = bf16[1280,2048]{1,0:T(8,128)(2,1)} async-done(((bf16[320,2048]{1,0:T(8,128)(2,1)}), bf16[1280,2048]{1,0:T(8,128)(2,1)}) %all-gather.5.cloned.1.call-update) | async-done | bytes 5242896 | tf_op jit(solution)/shard_map/all_gather | solution.py:59
  261.8 7.9 %copy.35 = bf16[1280,2048]{0,1:T(8,128)(2,1)} copy(bf16[1280,2048]{1,0:T(8,128)(2,1)} %all-gather.5.cloned.1.call-done) | data formatting | bytes 10485760 | tf_op jit(solution)/shard_map/all_gather | solution.py:59
  269.7 0.0 copy-start.1
  269.7 13.5 %fusion.17 = bf16[16,40,8,128]{3,2,1,0:T(8,128)(2,1)S(1)} fusion(bf16[1280,16,128]{0,2,1:T(8,128)(2,1)} %bitcast.106, f32[16,320,1280]{2,1,0:T(8,128)} %get-tuple-element.12, f32[16,320]{1,0:T(8,128)S(1)} %broadcast_maximum_fusion, pred[320,1280]{1,0:T(8,128)(4,1)S(1)} %fusion.16, f32[320,16]{0,1:T(8,128)S(1)} %bitcast.109), kind=kOutput, calls=%fused_computation.23 | convolution fusion | flops 1711800320 | bytes 33218560 | tf_op jit(solution)/shard_map/hqk,khd->qhd/dot_general | solution.py:76
  283.2 1.4 copy.94
  284.6 0.0 copy-done.1
  (6 shorter events, 0.0 us)
Async XLA Ops:
  7.2 163.9 %copy-start = (bf16[320,2048]{1,0:T(8,128)(2,1)S(1)}, bf16[320,2048]{1,0:T(8,128)(2,1)}, u32[]{:S(2)}) copy-start(bf16[320,2048]{1,0:T(8,128)(2,1)} %param.13) | copy-start | bytes 3932164
  7.2 57.6 %all-gather.9.cloned.1.call-start = ((), (), s32[]{:S(2)}) async-start(), calls=%async_computation.2 | async-start | bytes 2621440 | tf_op jit(solution)/shard_map/all_gather | solution.py:25
  12.5 4.9 %copy-start.4 = (s32[320]{0:T(512)S(1)}, s32[320]{0:T(512)}, u32[]{:S(2)}) copy-start(s32[320]{0:T(512)} %param.15) | copy-start | bytes 3844
  12.5 15.9 %copy-start.5 = (bf16[2048]{0:T(1024)(128)(2,1)S(1)}, bf16[2048]{0:T(1024)(128)(2,1)}, u32[]{:S(2)}) copy-start(bf16[2048]{0:T(1024)(128)(2,1)} %param.11) | copy-start | bytes 12292
  15.9 51.1 %copy-start.3 = (bf16[320,2048]{1,0:T(8,128)(2,1)S(1)}, bf16[320,2048]{1,0:T(8,128)(2,1)}, u32[]{:S(2)}) copy-start(bf16[320,2048]{1,0:T(8,128)(2,1)} %param.8) | copy-start | bytes 3932164
  16.0 147.2 %all-gather.7.cloned.1.call-start = ((), (), s32[]{:S(2)}) async-start(), calls=%async_computation.1 | async-start | bytes 6553600 | tf_op jit(solution)/shard_map/all_gather | solution.py:55
  16.7 245.0 %all-gather.5.cloned.1.call-start = ((), (), s32[]{:S(2)}) async-start(), calls=%async_computation | async-start | bytes 6553600 | tf_op jit(solution)/shard_map/all_gather | solution.py:59
  69.7 7.2 %copy-start.2 = (bf16[320,2048]{1,0:T(8,128)(2,1)S(1)}, bf16[320,2048]{1,0:T(8,128)(2,1)}, u32[]{:S(2)}) copy-start(bf16[320,2048]{1,0:T(8,128)(2,1)} %param.12) | copy-start | bytes 3932164
  269.7 15.0 %copy-start.1 = (bf16[320,2048]{1,0:T(8,128)(2,1)S(1)}, bf16[320,2048]{1,0:T(8,128)(2,1)}, u32[]{:S(2)}) copy-start(bf16[320,2048]{1,0:T(8,128)(2,1)} %param.13) | copy-start | bytes 3932164
Sparse Core Ops, SparseCore 0:
  16.1 48.6 all-gather.8
  66.3 96.7 all-gather.6
  165.3 96.4 all-gather.4
where the time goes:
time: 292 us; the launch traced here: 291 us
  waiting for transfers between devices  183 us (63%)
  matrix products  40.1 us (14%)
  other arithmetic  22.5 us (8%)
  local copies, waits for them, and re-layouts  20.9 us (7%)
  between operations  14.5 us (5%)
  blocking collectives  10.1 us (3%)
    all_gather x1, waiting for transfers between devices, per_device(): key_flat = lax.all_gather(soft_key, 'seq', axis=0, tiled=True)  82.6 us
    all_gather x1, waiting for transfers between devices, per_device(): lax.all_gather(lin_out, 'seq', axis=0, tiled=True)  63.4 us
    all_gather x1, waiting for transfers between devices, per_device(): lax.all_gather(local_state[None].astype(jnp.bfloat16), 'seq', axis=0, til...  36.1 us
    reduce_sum x1, other arithmetic, per_device(): denom_sum = jnp.sum(probs, axis=-1)  13.9 us
    dot_general x1, matrix products, per_device(): jnp.einsum('hqk,khd->qhd', probs.astype(jnp.bfloat16), value_part, prefer...  13.5 us
    dot_general x1, matrix products, per_device(): jnp.einsum('qhd,khd->hqk', query_soft, key_part, preferred_element_type=j...  13.3 us
    unnamed x1, blocking collectives  10.1 us
    all_gather x1, local copies, waits for them, and re-layouts, per_device(): key_flat = lax.all_gather(soft_key, 'seq', axis=0, tiled=True)  7.92 us
  transfers between devices with their start and end apart: 3, of which 3 were waited for; matrix products, arithmetic and copies ran while one was open for 18% of the time, Pallas kernels for 0%

commit v1 on v0

--- a/solution.py
+++ b/solution.py
@@ -6,6 +6,26 @@
 
 HD = 128
 norm_eps = 1e-06
+
+
+def words_refer(my_tile, array_axis):
+    next_value = list(my_tile.shape[1:])
+    next_value[array_axis] *= my_tile.shape[0]
+    return jnp.moveaxis(my_tile, 0, array_axis).reshape(next_value)
+
+
+def roads_refer(chunk, comm_axis):
+    small = chunk[None]
+    n_shards = lax.axis_size(comm_axis)
+    for j in range(n_shards.bit_length() - 1):
+        local_now = 1 << j
+        mid_arr = map(lambda h: (h, h ^ local_now), range(n_shards))
+        e_next = list(mid_arr)
+        fresh = lax.ppermute(small, comm_axis, e_next)
+        even = jnp.stack([small, fresh])
+        long_array = lax.axis_index(comm_axis) >> j & 1
+        small = jnp.where(long_array == 0, even, even[::-1]).reshape(-1, *chunk.shape)
+    return small
 
 
 def per_device(lin_query, lin_key, lin_value, norm_gain, out_gate, soft_query, soft_key, doc_id):
@@ -56,9 +76,12 @@
     row_max = jnp.full((head_count, row_count), -1e30, jnp.float32)
     piece_rows = key_flat.shape[0]
     key_part = key_flat.reshape(piece_rows, head_count, HD)
-    value_part = lax.all_gather(lin_out, "seq", axis=0, tiled=True).reshape(
-        piece_rows, head_count, HD
-    )
+
+    def _guide_shards(local, inner_x, dim_no):
+        before = roads_refer(local, inner_x)
+        return words_refer(before, dim_no)
+
+    value_part = _guide_shards(lin_out, inner_x="seq", dim_no=0).reshape(piece_rows, head_count, HD)
     key_pos = jnp.arange(piece_rows, dtype=jnp.int32)
     logits = (
         jnp.einsum("qhd,khd->hqk", query_soft, key_part, preferred_element_type=jnp.float32)

time: 292 us -> 368 us (1.26)
  waiting for transfers between devices: 183 us -> 244 us
  other arithmetic: 22.5 us -> 31.4 us
  local copies, waits for them, and re-layouts: 20.9 us -> 26.8 us
    ppermute x0 -> x2, waiting for transfers between devices: none -> 208 us  [roads_refer(): fresh = lax.ppermute(small, comm_axis, e_next)]
    all_gather x1, waiting for transfers between devices: 82.6 us -> 0.01 us  [per_device(): key_flat = lax.all_gather(soft_key, 'seq', axis=0, tiled=True)]
    all_gather x1 -> x0, waiting for transfers between devices: 63.4 us -> none  [per_device(): lax.all_gather(lin_out, 'seq', axis=0, tiled=True)]
    all_gather x1 -> x0, local copies, waits for them, and re-layouts: 7.92 us -> none  [per_device(): lax.all_gather(lin_out, 'seq', axis=0, tiled=True)]
    another operation x0 -> x3, other arithmetic: none -> 7.63 us  [roads_refer(): even = jnp.stack([small, fresh])]
    another operation x0 -> x2, local copies, waits for them, and re-layouts: none -> 6.47 us  [the longest x1 3.25 us: roads_refer(): small = chunk[None]]
    unnamed x16 -> x17, local copies, waits for them, and re-layouts: 1.65 us -> 5.81 us
  transfers between devices with their start and end apart: 3 -> 4, of which waited for: 3 -> 3; matrix products, arithmetic and copies ran while one was open for 18% -> 11% of each run, Pallas kernels for 0% -> 0%
where the time goes in v1:
time: 368 us; the launch traced here: 367 us
  waiting for transfers between devices  244 us (66%)
  matrix products  39.2 us (11%)
  other arithmetic  31.4 us (9%)
  local copies, waits for them, and re-layouts  26.8 us (7%)
  between operations  14.8 us (4%)
  blocking collectives  10.1 us (3%)
    ppermute x2, waiting for transfers between devices, roads_refer(): fresh = lax.ppermute(small, comm_axis, e_next)  208 us
    all_gather x1, waiting for transfers between devices, per_device(): lax.all_gather(local_state[None].astype(jnp.bfloat16), 'seq', axis=0, til...  36 us
    reduce_sum x1, other arithmetic, per_device(): denom_sum = jnp.sum(probs, axis=-1)  13.9 us
    dot_general x1, matrix products, per_device(): jnp.einsum('hqk,khd->qhd', probs.astype(jnp.bfloat16), value_part, prefer...  13.7 us
    dot_general x1, matrix products, per_device(): jnp.einsum('qhd,khd->hqk', query_soft, key_part, preferred_element_type=j...  12.9 us
    unnamed x1, blocking collectives  10.1 us
    all_gather x1, local copies, waits for them, and re-layouts, per_device(): key_flat = lax.all_gather(soft_key, 'seq', axis=0, tiled=True)  7.92 us
    another operation x3, other arithmetic, roads_refer(): even = jnp.stack([small, fresh])  7.63 us
  transfers between devices with their start and end apart: 4, of which 3 were waited for; matrix products, arithmetic and copies ran while one was open for 11% of the time, Pallas kernels for 0%

profile of v1, /device:TPU:0, one launch (start us, length us, event | category | flops | bytes accessed | tf_op | source)
XLA Modules:
  0.0 367.1 jit_solution(5341161332522698862)
XLA Ops:
  7.2 0.0 copy-start
  7.2 0.0 all-gather.6.cloned.1.call-start
  7.2 1.3 dynamic-slice
  8.6 2.0 fusion.58
  10.6 2.0 broadcast_compare_fusion.1
  12.5 0.0 copy-start.4
  12.5 0.0 copy-start.5
  12.5 3.4 fusion.40
  15.9 0.0 copy-start.3
  15.9 0.0 all-gather.6.cloned.1.call-update
  16.0 0.0 all-gather.4.cloned.1.call-start
  16.0 0.7 all-gather.4.cloned.1.call-update
  16.7 0.0 copy-done.4
  16.7 0.1 fusion.52
  17.5 0.0 copy-done.5
  17.5 0.3 dynamic-update-slice.1
  17.8 10.1 %all-reduce.2 = (s32[4]{0:T(128)S(1)}, s32[1280]{0:T(1024)S(1)}) all-reduce(s32[4]{0:T(128)S(1)} %get-tuple-element.9, s32[1280]{0:T(1024)S(1)} %dynamic-update-slice.1), channel_id=1, replica_groups=mesh['grp'=2,'seq'=4,'head'=4] {'seq'}, use_global_device_ids=true, to_apply=%add | all-reduce | flops 1284 | bytes 10272
  27.9 0.6 compare_and_fusion
  28.6 36.0 %all-gather.6.cloned.1.call-done = bf16[64,128,128]{2,1,0:T(8,128)(2,1)} async-done(((bf16[16,128,128]{2,1,0:T(8,128)(2,1)}), bf16[64,128,128]{2,1,0:T(8,128)(2,1)}) %all-gather.6.cloned.1.call-update) | async-done | bytes 2097168 | tf_op jit(solution)/shard_map/all_gather | solution.py:45
  64.5 2.2 fusion.7
  66.8 0.0 copy-done.3
  66.8 2.7 fusion.35
  69.5 6.5 %multiply_reduce_fusion = (f32[320,16]{0,1:T(8,128)S(1)}, f32[320,16,128]{2,0,1:T(8,128)}) fusion(f32[16,128,320]{1,2,0:T(8,128)} %fusion.35, pred[320]{0:T(512)(128)(4,1)S(1)} %get-tuple-element.6, pred[320,320]{1,0:T(8,128)(4,1)S(1)} %fusion.52, bf16[320,2048]{1,0:T(8,128)(2,1)} %param.10, bf16[320,2048]{1,0:T(8,128)(2,1)} %param.9, ...), kind=kOutput, calls=%fused_computation.25 | convolution fusion | flops 844753920 | bytes 9298240 | tf_op jit(solution)/shard_map/hqk,khd->qhd/dot_general | solution.py:59
  75.9 2.7 fusion.13
  78.7 1.9 copy.35
  80.6 3.2 broadcast_in_dim_reshape.4
  83.8 0.2 collective-permute-start
  84.0 3.2 stack_broadcast_in_dim_reshape.3
  87.3 94.5 %collective-permute-done = bf16[1,320,2048]{2,1,0:T(8,128)(2,1)} collective-permute-done((bf16[1,320,2048]{2,1,0:T(8,128)(2,1)}, bf16[1,320,2048]{2,1,0:T(8,128)(2,1)}, u32[]{:S(2)}, u32[]{:S(2)}) %collective-permute-start) | collective-permute-done | bytes 1310752 | tf_op jit(solution)/shard_map/ppermute | solution.py:24
  181.8 2.0 pad_maximum_fusion.1
  183.7 3.5 fusion.16
  187.2 0.0 collective-permute-start.1
  187.2 0.0 copy-start.2
  187.2 0.4 fusion.21
  187.6 1.3 copy_bitcast_fusion.1
  188.9 113.3 %collective-permute-done.1 = bf16[2,320,2048]{2,1,0:T(8,128)(2,1)} collective-permute-done((bf16[2,320,2048]{2,1,0:T(8,128)(2,1)}, bf16[2,320,2048]{2,1,0:T(8,128)(2,1)}, u32[]{:S(2)}, u32[]{:S(2)}) %collective-permute-start.1) | collective-permute-done | bytes 2621472 | tf_op jit(solution)/shard_map/ppermute | solution.py:24
  302.1 0.0 copy-done.2
  302.1 2.2 pad_maximum_fusion
  304.4 1.8 reverse_select_fusion
  306.2 4.2 %copy.51 = bf16[160,8,16,128]{3,2,1,0:T(8,128)(2,1)} copy(bf16[160,8,16,128]{3,1,2,0:T(8,128)(2,1)S(1)} %bitcast.110) | data formatting | bytes 10485760
  310.3 0.0 all-gather.4.cloned.1.call-done
  310.3 7.9 %copy.38 = bf16[1280,2048]{0,1:T(8,128)(2,1)} copy(bf16[1280,2048]{1,0:T(8,128)(2,1)} %all-gather.4.cloned.1.call-done) | data formatting | bytes 10485760 | tf_op jit(solution)/shard_map/all_gather | solution.py:75
  318.2 0.0 copy-done
  318.2 12.9 %fusion = (f32[16,320]{1,0:T(8,128)S(1)}, f32[16,320,1280]{2,1,0:T(8,128)}) fusion(pred[320,1280]{1,0:T(8,128)(4,1)S(1)} %fusion.21, bf16[1280,16,128]{0,2,1:T(8,128)(2,1)} %bitcast.109, bf16[320,2048]{1,0:T(8,128)(2,1)S(1)} %copy-done), kind=kOutput, calls=%fused_computation.2 | convolution fusion | flops 1697377280 | bytes 33198080 | tf_op jit(solution)/shard_map/qhd,khd->hqk/dot_general | solution.py:87
  331.2 13.9 %fusion.1 = f32[16,320]{1,0:T(8,128)S(1)} fusion(f32[16,320,1280]{2,1,0:T(8,128)} %get-tuple-element.14, f32[16,320]{1,0:T(8,128)S(1)} %broadcast_maximum_fusion, pred[320,1280]{1,0:T(8,128)(4,1)S(1)} %fusion.21), kind=kLoop, calls=%fused_computation.3 | loop fusion | flops 32762880 | bytes 26664960 | tf_op jit(solution)/shard_map/reduce_sum | solution.py:98
  345.0 0.0 copy-start.1
  345.1 13.7 %fusion.22 = bf16[16,40,8,128]{3,2,1,0:T(8,128)(2,1)S(1)} fusion(bf16[1280,16,128]{2,1,0:T(8,128)(2,1)} %bitcast.111, f32[16,320,1280]{2,1,0:T(8,128)} %get-tuple-element.14, f32[16,320]{1,0:T(8,128)S(1)} %broadcast_maximum_fusion, pred[320,1280]{1,0:T(8,128)(4,1)S(1)} %fusion.21, f32[320,16]{0,1:T(8,128)S(1)} %bitcast.114), kind=kOutput, calls=%fused_computation.30 | convolution fusion | flops 1711800320 | bytes 33218560 | tf_op jit(solution)/shard_map/hqk,khd->qhd/dot_general | solution.py:99
  358.8 1.4 copy.99
  360.2 0.0 copy-done.1
  (6 shorter events, 0.0 us)
Async XLA Ops:
  7.2 311.1 %copy-start = (bf16[320,2048]{1,0:T(8,128)(2,1)S(1)}, bf16[320,2048]{1,0:T(8,128)(2,1)}, u32[]{:S(2)}) copy-start(bf16[320,2048]{1,0:T(8,128)(2,1)} %param.13) | copy-start | bytes 3932164
  7.2 57.4 %all-gather.6.cloned.1.call-start = ((), (), s32[]{:S(2)}) async-start(), calls=%async_computation.1 | async-start | bytes 2621440 | tf_op jit(solution)/shard_map/all_gather | solution.py:45
  12.5 4.2 %copy-start.4 = (s32[320]{0:T(512)S(1)}, s32[320]{0:T(512)}, u32[]{:S(2)}) copy-start(s32[320]{0:T(512)} %param.15) | copy-start | bytes 3844
  12.5 5.0 %copy-start.5 = (bf16[2048]{0:T(1024)(128)(2,1)S(1)}, bf16[2048]{0:T(1024)(128)(2,1)}, u32[]{:S(2)}) copy-start(bf16[2048]{0:T(1024)(128)(2,1)} %param.11) | copy-start | bytes 12292
  15.9 50.8 %copy-start.3 = (bf16[320,2048]{1,0:T(8,128)(2,1)S(1)}, bf16[320,2048]{1,0:T(8,128)(2,1)}, u32[]{:S(2)}) copy-start(bf16[320,2048]{1,0:T(8,128)(2,1)} %param.8) | copy-start | bytes 3932164
  16.0 294.4 %all-gather.4.cloned.1.call-start = ((), (), s32[]{:S(2)}) async-start(), calls=%async_computation | async-start | bytes 6553600 | tf_op jit(solution)/shard_map/all_gather | solution.py:75
  83.8 97.9 %collective-permute-start = (bf16[1,320,2048]{2,1,0:T(8,128)(2,1)}, bf16[1,320,2048]{2,1,0:T(8,128)(2,1)}, u32[]{:S(2)}, u32[]{:S(2)}) collective-permute-start(bf16[1,320,2048]{2,1,0:T(8,128)(2,1)} %broadcast_in_dim_reshape.4), channel_id=1, source_target_pairs={{0,4},{4,0},{8,12},{12,8},{1,5},{5,1},{9,13},{13,9},{2,6},{6,2},{1... | collective-permute-start | bytes 3932168 | tf_op jit(solution)/shard_map/ppermute | solution.py:24
  187.2 115.0 %collective-permute-start.1 = (bf16[2,320,2048]{2,1,0:T(8,128)(2,1)}, bf16[2,320,2048]{2,1,0:T(8,128)(2,1)}, u32[]{:S(2)}, u32[]{:S(2)}) collective-permute-start(bf16[2,320,2048]{2,1,0:T(8,128)(2,1)} %get-tuple-element.5), channel_id=1, source_target_pairs={{0,8},{4,12},{8,0},{12,4},{1,9},{5,13},{9,1},{13,5},{2,10},{6,14},... | collective-permute-start | bytes 7864328 | tf_op jit(solution)/shard_map/ppermute | solution.py:24
  187.2 114.9 %copy-start.2 = (bf16[1,2,320,2048]{3,2,1,0:T(8,128)(2,1)S(1)}, bf16[1,2,320,2048]{3,2,1,0:T(8,128)(2,1)}, u32[]{:S(2)}) copy-start(bf16[1,2,320,2048]{3,2,1,0:T(8,128)(2,1)} %get-tuple-element.4) | copy-start | bytes 7864324
  345.0 15.2 %copy-start.1 = (bf16[320,2048]{1,0:T(8,128)(2,1)S(1)}, bf16[320,2048]{1,0:T(8,128)(2,1)}, u32[]{:S(2)}) copy-start(bf16[320,2048]{1,0:T(8,128)(2,1)} %param.13) | copy-start | bytes 3932164
Sparse Core Ops, SparseCore 0:
  16.1 48.4 all-gather.5
  66.1 122.9 all-gather.3
